TPU v7x, 32 devices: a whole 2x2x4 slice. The times are simulated.
32 devices in a mesh: groups: 2 (over y), dom: 4 (over x, core), sub: 4 (over z).
Axes of the slice: x: 2, y: 2, z: 4, core: 2. Of those that a mesh axis runs over, the one named last changes fastest.
Arguments:
- node_states: float32 [8192, 512], P(('groups', 'dom', 'sub')), parts along dimension 0, may hold values from -6 to 6
- node_pre: float32 [8192, 512], P(('groups', 'dom', 'sub')), parts along dimension 0, may hold values from -6 to 6
- edge_states: float32 [4096, 512], P(('groups', 'dom', 'sub')), parts along dimension 0, may hold values from -6 to 6
- edge_pre: float32 [4096, 512], P(('groups', 'dom', 'sub')), parts along dimension 0, may hold values from -6 to 6
- node_cotangent: float32 [8192, 512], P(('groups', 'dom', 'sub')), parts along dimension 0, may hold values from -6 to 6
- edge_cotangent: float32 [4096, 512], P(('groups', 'dom', 'sub')), parts along dimension 0, may hold values from -6 to 6
- endpoints: int32 [2, 4096], P(None, ('groups', 'dom', 'sub')), parts along dimension 1, may hold values from 0 to 319, as said below
- send_lists: int32 [32, 4, 16], P(('groups', 'dom', 'sub')), parts along dimension 0, may hold values from 0 to 255, as said below
- node_counts: int32 [32], P(('groups', 'dom', 'sub')), parts along dimension 0, may hold values from 128 to 256
- edge_blocks: int32 [32], P(('groups', 'dom', 'sub')), parts along dimension 0, may hold values from 1 to 1
- edge_first: float32 [1536, 512], P(('dom', 'sub')), may hold values from -0.15625 to 0.15625
- edge_second: float32 [512, 512], P(('dom', 'sub')), may hold values from -0.25 to 0.25
- edge_bias: float32 [512], P(('dom', 'sub')), may hold values from -3 to 3
- edge_gain: float32 [512], P(('dom', 'sub')), may hold values from 0.5 to 1.5
- edge_shift: float32 [512], P(('dom', 'sub')), may hold values from -3 to 3
- node_first: float32 [1024, 512], P(('dom', 'sub')), may hold values from -0.1875 to 0.1875
- node_second: float32 [512, 512], P(('dom', 'sub')), may hold values from -0.25 to 0.25
- node_bias: float32 [512], P(('dom', 'sub')), may hold values from -3 to 3
- node_gain: float32 [512], P(('dom', 'sub')), may hold values from 0.5 to 1.5
Outputs:
- edge_grads: float32 [4096, 512], P(('groups', 'dom', 'sub')), parts along dimension 0
- node_grads: float32 [8192, 512], P(('groups', 'dom', 'sub')), parts along dimension 0
- edge_first_grad: float32 [3072, 512], P(('groups', 'dom', 'sub')), parts along dimension 0
- edge_second_grad: float32 [1024, 512], P(('groups', 'dom', 'sub')), parts along dimension 0
- node_first_grad: float32 [2048, 512], P(('groups', 'dom', 'sub')), parts along dimension 0
- node_second_grad: float32 [1024, 512], P(('groups', 'dom', 'sub')), parts along dimension 0
There are 2 independent parts, one for each index of `groups`. A program takes and returns all parts, laid end to end along the dimension named above; an argument that names none is the same for every part. Nothing has to cross between parts.
Inputs may be any that keep to these rules, and one draw needn't show every extreme that they name: `endpoints`: sender slots are a live local node below node_counts of the device, or a ghost slot 256 + k * 16 + j whose neighbour k exists; receiver slots are live local nodes. `send_lists`: every entry is a live node of its device.
All inputs are finite; a program needn't handle non-finite values.
Results may differ from a plain program's by a relative error of at most 0.0003.
Values sent between devices are 32-bit elements; how exact they have to be, the bound alone decides.
No kernel may reach another device: no remote copies, remote signals or barrier semaphores. Data moves between devices by JAX's collectives and lax.ppermute only.
A program may use at most 128 MiB of HBM per device.

v0:
```python
import math
import jax
import jax.numpy as jnp
from jax import lax
from jax.sharding import PartitionSpec as P

EPSILON = 1e-05


def padded(cells, sides, width):
    for axis, dim in sides:
        count = lax.axis_size(axis)
        ends = count - 1
        head = lax.slice_in_dim(cells, 0, width, axis=dim)
        tail = lax.slice_in_dim(cells, cells.shape[dim] - width, cells.shape[dim], axis=dim)
        cells = jnp.concatenate(
            [
                lax.ppermute(tail, axis, [(i, (i + 1) % count) for i in range(ends)]),
                cells,
                lax.ppermute(head, axis, [((i + 1) % count, i) for i in range(ends)]),
            ],
            axis=dim,
        )
    return cells


def matmul(left, right):
    return jnp.dot(left, right, precision=lax.Precision.HIGHEST, preferred_element_type=jnp.float32)


def inner(left, right):
    return lax.dot_general(
        left,
        right,
        (((0,), (0,)), ((), ())),
        precision=lax.Precision.HIGHEST,
        preferred_element_type=jnp.float32,
    )


def outer_back(left, right):
    return lax.dot_general(
        left,
        right,
        (((1,), (1,)), ((), ())),
        precision=lax.Precision.HIGHEST,
        preferred_element_type=jnp.float32,
    )


def layer_norm(values):
    center = values - jnp.mean(values, axis=-1, keepdims=True)
    inverse = 1.0 / jnp.sqrt(jnp.mean(center * center, axis=-1, keepdims=True) + EPSILON)
    return (center * inverse, inverse)


def norm_back(upstream, normed, inverse):
    first = jnp.mean(upstream, axis=-1, keepdims=True)
    second = jnp.mean(upstream * normed, axis=-1, keepdims=True)
    return inverse * (upstream - first - normed * second)


def shards(
    node_states,
    node_pre,
    edge_states,
    edge_pre,
    node_cotangent,
    edge_cotangent,
    endpoints,
    send_lists,
    node_counts,
    edge_blocks,
    edge_first,
    edge_second,
    edge_bias,
    edge_gain,
    edge_shift,
    node_first,
    node_second,
    node_bias,
    node_gain,
):
    node_rows, width = node_states.shape
    edge_rows = edge_states.shape[0]
    ghost = send_lists.shape[2]
    dom_count = lax.axis_size("dom")
    sub_count = lax.axis_size("sub")
    peer_count = dom_count * sub_count
    lists = send_lists[0]
    outgoing = jnp.take(node_states, lists.reshape(-1), axis=0).reshape(4, ghost, width)
    dom_side = padded(jnp.stack([outgoing[1], outgoing[0]]), (("dom", 0),), 1)
    sub_side = padded(jnp.stack([outgoing[3], outgoing[2]]), (("sub", 0),), 1)
    ghosts = jnp.stack([dom_side[0], dom_side[3], sub_side[0], sub_side[3]])
    ghosts = ghosts.reshape(4 * ghost, width)
    full_node_first, full_node_second, full_node_bias, full_node_gain = (
        lax.all_gather(node_first, ("dom", "sub"), axis=0, tiled=True),
        lax.all_gather(node_second, ("dom", "sub"), axis=0, tiled=True),
        lax.all_gather(node_bias, ("dom", "sub"), axis=0, tiled=True),
        lax.all_gather(node_gain, ("dom", "sub"), axis=0, tiled=True),
    )
    full_edge_first, full_edge_second, full_edge_bias, full_edge_gain, full_edge_shift = (
        lax.all_gather(edge_first, ("dom", "sub"), axis=0, tiled=True),
        lax.all_gather(edge_second, ("dom", "sub"), axis=0, tiled=True),
        lax.all_gather(edge_bias, ("dom", "sub"), axis=0, tiled=True),
        lax.all_gather(edge_gain, ("dom", "sub"), axis=0, tiled=True),
        lax.all_gather(edge_shift, ("dom", "sub"), axis=0, tiled=True),
    )
    live_nodes = (jnp.arange(node_rows) < node_counts[0]).astype(jnp.float32)[:, None]
    live_edges = (jnp.arange(edge_rows) < edge_blocks[0] * 128).astype(jnp.float32)[:, None]
    source = endpoints[0]
    target = endpoints[1]
    edge_scale = 1.0 / math.sqrt(edge_rows * peer_count)
    node_scale = 1.0 / math.sqrt(node_rows * peer_count)
    edge_act = jnp.maximum(edge_pre, 0.0)
    edge_normed, edge_inverse = layer_norm(matmul(edge_act, full_edge_second) + full_edge_bias)
    message = (edge_normed * full_edge_gain + full_edge_shift) * live_edges
    aggregate = jax.ops.segment_sum(message, target, node_rows)
    node_act = jnp.maximum(node_pre, 0.0)
    node_normed, node_inverse = layer_norm(matmul(node_act, full_node_second) + full_node_bias)
    node_upstream = node_cotangent * live_nodes
    node_grad_z = norm_back(node_upstream * full_node_gain, node_normed, node_inverse)
    node_grad_pre = outer_back(node_grad_z, full_node_second) * (node_pre > 0).astype(jnp.float32)
    node_input = jnp.concatenate([node_states, aggregate], axis=1)
    node_first_grad, node_second_grad = (
        lax.psum_scatter(
            inner(node_input, node_grad_pre) * node_scale,
            ("dom", "sub"),
            scatter_dimension=0,
            tiled=True,
        ),
        lax.psum_scatter(
            inner(node_act, node_grad_z) * node_scale,
            ("dom", "sub"),
            scatter_dimension=0,
            tiled=True,
        ),
    )
    node_grad_input = outer_back(node_grad_pre, full_node_first)
    state_grads = node_upstream + node_grad_input[:, :width]
    edge_upstream = (
        edge_cotangent + jnp.take(node_grad_input[:, width:], target, axis=0)
    ) * live_edges
    edge_grad_z = norm_back(edge_upstream * full_edge_gain, edge_normed, edge_inverse)
    edge_grad_pre = outer_back(edge_grad_z, full_edge_second) * (edge_pre > 0).astype(jnp.float32)
    edge_second_grad = lax.psum_scatter(
        inner(edge_act, edge_grad_z) * edge_scale, ("dom", "sub"), scatter_dimension=0, tiled=True
    )
    extended = jnp.concatenate([node_states, ghosts], axis=0)
    features = jnp.concatenate(
        [edge_states, jnp.take(extended, source, axis=0), jnp.take(extended, target, axis=0)],
        axis=1,
    )
    edge_first_grad = lax.psum_scatter(
        inner(features, edge_grad_pre) * edge_scale, ("dom", "sub"), scatter_dimension=0, tiled=True
    )
    edge_grad_input = outer_back(edge_grad_pre, full_edge_first)
    edge_grads = (edge_cotangent + edge_grad_input[:, :width]) * live_edges
    extended_grads = jax.ops.segment_sum(
        edge_grad_input[:, width : 2 * width], source, node_rows + 4 * ghost
    )
    extended_grads = extended_grads + jax.ops.segment_sum(
        edge_grad_input[:, 2 * width :], target, node_rows + 4 * ghost
    )
    state_grads = state_grads + extended_grads[:node_rows]
    ghost_grads = extended_grads[node_rows:].reshape(4, ghost, width)
    dom_back = padded(jnp.stack([ghost_grads[0], ghost_grads[1]]), (("dom", 0),), 1)
    sub_back = padded(jnp.stack([ghost_grads[2], ghost_grads[3]]), (("sub", 0),), 1)
    returned = jnp.stack([dom_back[3], dom_back[0], sub_back[3], sub_back[0]])
    state_grads = state_grads + jax.ops.segment_sum(
        returned.reshape(-1, width), lists.reshape(-1), node_rows
    )
    return (
        edge_grads,
        state_grads,
        edge_first_grad,
        edge_second_grad,
        node_first_grad,
        node_second_grad,
    )


def solution(mesh):
    in_specs = (
        P(("groups", "dom", "sub"), None),
        P(("groups", "dom", "sub"), None),
        P(("groups", "dom", "sub"), None),
        P(("groups", "dom", "sub"), None),
        P(("groups", "dom", "sub"), None),
        P(("groups", "dom", "sub"), None),
        P(None, ("groups", "dom", "sub")),
        P(("groups", "dom", "sub"), None, None),
        P(("groups", "dom", "sub")),
        P(("groups", "dom", "sub")),
        P(("dom", "sub"), None),
        P(("dom", "sub"), None),
        P(("dom", "sub")),
        P(("dom", "sub")),
        P(("dom", "sub")),
        P(("dom", "sub"), None),
        P(("dom", "sub"), None),
        P(("dom", "sub")),
        P(("dom", "sub")),
    )
    out_specs = (
        P(("groups", "dom", "sub"), None),
        P(("groups", "dom", "sub"), None),
        P(("groups", "dom", "sub"), None),
        P(("groups", "dom", "sub"), None),
        P(("groups", "dom", "sub"), None),
        P(("groups", "dom", "sub"), None),
    )
    return jax.shard_map(shards, mesh=mesh, in_specs=in_specs, out_specs=out_specs, check_vma=False)
```

profile of v0, /device:TPU:0, one launch (start us, length us, event | category | flops | bytes accessed | tf_op | source)
XLA Modules:
  0.0 442.2 jit_solution(13776215325105201834)
XLA Ops:
  7.2 0.7 all-gather.7.cloned.1.call-update
  8.0 0.7 all-gather.5.cloned.1.call-update
  8.7 0.7 all-gather.9.cloned.1.call-update
  10.7 1.2 dynamic-slice
  12.6 0.9 dynamic-update-slice
  13.4 0.8 dynamic-update-slice.1
  14.3 0.8 dynamic-update-slice.2
  15.1 0.8 dynamic-update-slice.3
  16.0 0.8 dynamic-update-slice.4
  16.8 63.6 %all-reduce.5 = (f32[512]{0:T(512)S(1)}, f32[512]{0:T(512)S(1)}, f32[512]{0:T(512)S(1)}, f32[512]{0:T(512)S(1)}, f32[512]{0:T(512)S(1)}) all-reduce(f32[512]{0:T(512)S(1)} %dynamic-update-slice.1, f32[512]{0:T(512)S(1)} %dynamic-update-slice.2, f32[512]{0:T(512)S(1)} %dynamic-update-slice.3, ...), channel_id=1, replica_groups=mesh['groups'=2,'dom'=4,'sub'=4] {'dom','sub'}, use_global_device_ids=true, to_apply=%add.1 | all-reduce | flops 2560 | bytes 20480
  80.4 2.5 fusion.44
  83.5 2.4 convolution_multiply_fusion.2
  86.7 3.5 all-gather.5.cloned.1.call-done
  90.2 2.0 fusion.43
  92.5 2.2 scatter_custom_fusion.2
  94.7 2.5 convolution_select_fusion
  97.3 3.2 convolution_multiply_fusion.1
  100.9 0.7 gather_fusion.1
  101.6 31.2 %all-gather.9.cloned.1.call-done = f32[1024,512]{1,0:T(8,128)} async-done(((f32[64,512]{1,0:T(8,128)}), f32[1024,512]{1,0:T(8,128)}) %all-gather.9.cloned.1.call-update) | async-done | bytes 2097168 | tf_op jit(solution)/shard_map/all_gather | solution.py:97
  132.8 3.5 fusion.45
  136.3 1.0 copy-done.5
  137.4 0.8 gather_fusion
  138.4 2.1 convolution_multiply_fusion.3
  140.6 2.2 collective-permute-start.4
  142.8 1.3 collective-permute-start.5
  144.1 2.4 collective-permute-start.6
  146.6 1.3 collective-permute-start.7
  147.9 0.7 collective-permute-done.6
  148.6 4.4 collective-permute-done.7
  153.0 0.8 gather_fusion.2
  153.8 1.5 gather_fusion.3
  155.2 1.1 broadcast_select_fusion
  156.3 1.2 convolution_select_fusion.1
  157.5 4.4 convolution_multiply_fusion
  162.0 17.1 %all-gather.11.cloned.1.call-done = f32[1536,512]{1,0:T(8,128)} async-done(((f32[96,512]{1,0:T(8,128)}), f32[1536,512]{1,0:T(8,128)}) %all-gather.11.cloned.1.call-update) | async-done | bytes 3145744 | tf_op jit(solution)/shard_map/all_gather | solution.py:103
  179.1 5.2 %fusion.46 = f32[128,1536]{1,0:T(8,128)S(1)} fusion(f32[128,512]{1,0:T(8,128)S(1)} %convolution_select_fusion.1, f32[1536,512]{1,0:T(8,128)} %all-gather.11.cloned.1.call-done), kind=kOutput, calls=%fused_computation.115 | convolution fusion | flops 1207959552 | bytes 4194304 | tf_op jit(solution)/shard_map/dot_general | solution.py:42
  184.3 0.8 fusion.42
  185.1 2.3 scatter_custom_fusion
  187.4 1.3 collective-permute-start
  188.7 3.0 collective-permute-start.1
  191.8 1.3 collective-permute-start.2
  193.1 4.5 %collective-permute-start.3 = (f32[1,16,512]{2,1,0:T(8,128)S(1)}, f32[1,16,512]{2,1,0:T(8,128)S(1)}, u32[]{:S(2)}, u32[]{:S(2)}) collective-permute-start(f32[1,16,512]{2,1,0:T(8,128)S(1)} %get-tuple-element.25), channel_id=1, source_target_pairs={{0,1},{1,2},{2,3},{4,5},{5,6},{6,7},{8,9},{9,10},{10,11},{12,13},{... | collective-permute-start | bytes 98312 | tf_op jit(solution)/shard_map/ppermute | solution.py:18
  197.8 1.4 collective-permute-done.3
  199.2 1.2 scatter_fusion
  200.4 38.9 %reduce-scatter.11.cloned.1.call-done = f32[32,512]{1,0:T(8,128)} async-done(((f32[512,512]{1,0:T(8,128)}), f32[32,512]{1,0:T(8,128)}) %reduce-scatter.11.cloned.1.call-update) | async-done | bytes 65552 | tf_op jit(solution)/shard_map/reduce_scatter | solution.py:132
  239.4 65.3 %reduce-scatter.9.cloned.1.call-done = f32[64,512]{1,0:T(8,128)} async-done(((f32[1024,512]{1,0:T(8,128)}), f32[64,512]{1,0:T(8,128)}) %reduce-scatter.9.cloned.1.call-update) | async-done | bytes 131088 | tf_op jit(solution)/shard_map/reduce_scatter | solution.py:126
  304.7 60.6 %reduce-scatter.7.cloned.1.call-done = f32[32,512]{1,0:T(8,128)} async-done(((f32[512,512]{1,0:T(8,128)}), f32[32,512]{1,0:T(8,128)}) %reduce-scatter.7.cloned.1.call-update) | async-done | bytes 65552 | tf_op jit(solution)/shard_map/reduce_scatter | solution.py:146
  365.3 70.1 %reduce-scatter.5.cloned.1.call-done = f32[96,512]{1,0:T(8,128)} async-done(((f32[1536,512]{1,0:T(8,128)}), f32[96,512]{1,0:T(8,128)}) %reduce-scatter.5.cloned.1.call-update) | async-done | bytes 196624 | tf_op jit(solution)/shard_map/reduce_scatter | solution.py:154
  (84 shorter events, 2.7 us)
Async XLA Ops:
  7.2 76.3 %copy-start.2 = (f32[256,512]{1,0:T(8,128)S(1)}, f32[256,512]{1,0:T(8,128)}, u32[]{:S(2)}) copy-start(f32[256,512]{1,0:T(8,128)} %param.22) | copy-start | bytes 1572868
  7.2 76.0 %copy-start.1 = (f32[256,512]{1,0:T(8,128)S(1)}, f32[256,512]{1,0:T(8,128)}, u32[]{:S(2)}) copy-start(f32[256,512]{1,0:T(8,128)} %param.25) | copy-start | bytes 1572868
  7.2 73.2 %all-gather.7.cloned.1.call-start = ((), (), s32[]{:S(2)}) async-start(), calls=%async_computation.5 | async-start | bytes 1114112 | tf_op jit(solution)/shard_map/all_gather | solution.py:98
  7.9 82.3 %all-gather.5.cloned.1.call-start = ((), (), s32[]{:S(2)}) async-start(), calls=%async_computation.4 | async-start | bytes 1114112 | tf_op jit(solution)/shard_map/all_gather | solution.py:104
  8.7 124.1 %all-gather.9.cloned.1.call-start = ((), (), s32[]{:S(2)}) async-start(), calls=%async_computation.6 | async-start | bytes 2228224 | tf_op jit(solution)/shard_map/all_gather | solution.py:97
  9.4 169.7 %all-gather.11.cloned.1.call-start = ((), (), s32[]{:S(2)}) async-start(), calls=%async_computation.7 | async-start | bytes 3342336 | tf_op jit(solution)/shard_map/all_gather | solution.py:103
  10.0 229.4 %reduce-scatter.11.cloned.1.call-start = ((), (), s32[]{:S(2)}) async-start(), calls=%async_computation.11 | async-start | bytes 1114112 | tf_op jit(solution)/shard_map/reduce_scatter | solution.py:132
  82.9 3.0 copy-start.13
  83.0 7.3 %copy-start.7 = (f32[128,512]{1,0:T(8,128)S(1)}, f32[128,512]{1,0:T(8,128)}, u32[]{:S(2)}) copy-start(f32[128,512]{1,0:T(8,128)} %param.24) | copy-start | bytes 786436
  85.9 11.3 %copy-start = (f32[256,512]{1,0:T(8,128)S(1)}, f32[256,512]{1,0:T(8,128)}, u32[]{:S(2)}) copy-start(f32[256,512]{1,0:T(8,128)} %param.21) | copy-start | bytes 1572868
  85.9 218.7 %reduce-scatter.9.cloned.1.call-start = ((), (), s32[]{:S(2)}) async-start(), calls=%async_computation.10 | async-start | bytes 2228224 | tf_op jit(solution)/shard_map/reduce_scatter | solution.py:126
  94.7 2.5 copy-start.8
  97.2 3.5 copy-start.12
  100.5 264.8 %reduce-scatter.7.cloned.1.call-start = ((), (), s32[]{:S(2)}) async-start(), calls=%async_computation.9 | async-start | bytes 1114112 | tf_op jit(solution)/shard_map/reduce_scatter | solution.py:146
  101.6 36.5 %copy-start.9 = (f32[128,512]{1,0:T(8,128)S(1)}, f32[128,512]{1,0:T(8,128)}, u32[]{:S(2)}) copy-start(f32[128,512]{1,0:T(8,128)} %param.26) | copy-start | bytes 786436
  136.3 1.0 copy-start.5
  140.5 294.9 %reduce-scatter.5.cloned.1.call-start = ((), (), s32[]{:S(2)}) async-start(), calls=%async_computation.8 | async-start | bytes 3342336 | tf_op jit(solution)/shard_map/reduce_scatter | solution.py:154
  140.6 7.2 %collective-permute-start.4 = (f32[1,16,512]{2,1,0:T(8,128)S(1)}, f32[1,16,512]{2,1,0:T(8,128)S(1)}, u32[]{:S(2)}, u32[]{:S(2)}) collective-permute-start(f32[1,16,512]{2,1,0:T(8,128)S(1)} %get-tuple-element.28), channel_id=1, source_target_pairs={{0,4},{4,8},{8,12},{1,5},{5,9},{9,13},{2,6},{6,10},{10,14},{3,7},{... | collective-permute-start | bytes 98312 | tf_op jit(solution)/shard_map/ppermute | solution.py:18
  142.8 5.1 %collective-permute-start.5 = (f32[1,16,512]{2,1,0:T(8,128)S(1)}, f32[1,16,512]{2,1,0:T(8,128)S(1)}, u32[]{:S(2)}, u32[]{:S(2)}) collective-permute-start(f32[1,16,512]{2,1,0:T(8,128)S(1)} %get-tuple-element.31), channel_id=1, source_target_pairs={{4,0},{8,4},{12,8},{5,1},{9,5},{13,9},{6,2},{10,6},{14,10},{7,3},{... | collective-permute-start | bytes 98312 | tf_op jit(solution)/shard_map/ppermute | solution.py:20
  144.1 4.4 %collective-permute-start.6 = (f32[1,16,512]{2,1,0:T(8,128)S(1)}, f32[1,16,512]{2,1,0:T(8,128)S(1)}, u32[]{:S(2)}, u32[]{:S(2)}) collective-permute-start(f32[1,16,512]{2,1,0:T(8,128)S(1)} %get-tuple-element.30), channel_id=1, source_target_pairs={{0,1},{1,2},{2,3},{4,5},{5,6},{6,7},{8,9},{9,10},{10,11},{12,13},{... | collective-permute-start | bytes 98312 | tf_op jit(solution)/shard_map/ppermute | solution.py:18
  146.6 6.4 %collective-permute-start.7 = (f32[1,16,512]{2,1,0:T(8,128)S(1)}, f32[1,16,512]{2,1,0:T(8,128)S(1)}, u32[]{:S(2)}, u32[]{:S(2)}) collective-permute-start(f32[1,16,512]{2,1,0:T(8,128)S(1)} %get-tuple-element.29), channel_id=1, source_target_pairs={{1,0},{2,1},{3,2},{5,4},{6,5},{7,6},{9,8},{10,9},{11,10},{13,12},{... | collective-permute-start | bytes 98312 | tf_op jit(solution)/shard_map/ppermute | solution.py:20
  153.0 3.3 copy-start.4
  155.2 2.3 copy-start.11
  161.9 22.4 %copy-start.10 = (f32[128,512]{1,0:T(8,128)S(1)}, f32[128,512]{1,0:T(8,128)}, u32[]{:S(2)}) copy-start(f32[128,512]{1,0:T(8,128)} %param.26) | copy-start | bytes 786436
  162.0 35.7 %copy-start.6 = (f32[256,1024]{1,0:T(8,128)S(1)}, f32[256,1024]{1,0:T(8,128)}, u32[]{:S(2)}) copy-start(f32[256,1024]{1,0:T(8,128)} %copy-done.5) | copy-start | bytes 3145732
  187.4 10.3 %collective-permute-start = (f32[1,16,512]{2,1,0:T(8,128)S(1)}, f32[1,16,512]{2,1,0:T(8,128)S(1)}, u32[]{:S(2)}, u32[]{:S(2)}) collective-permute-start(f32[1,16,512]{2,1,0:T(8,128)S(1)} %get-tuple-element.24), channel_id=1, source_target_pairs={{4,0},{8,4},{12,8},{5,1},{9,5},{13,9},{6,2},{10,6},{14,10},{7,3},{... | collective-permute-start | bytes 98312 | tf_op jit(solution)/shard_map/ppermute | solution.py:20
  188.7 9.1 %collective-permute-start.1 = (f32[1,16,512]{2,1,0:T(8,128)S(1)}, f32[1,16,512]{2,1,0:T(8,128)S(1)}, u32[]{:S(2)}, u32[]{:S(2)}) collective-permute-start(f32[1,16,512]{2,1,0:T(8,128)S(1)} %get-tuple-element.27), channel_id=1, source_target_pairs={{0,4},{4,8},{8,12},{1,5},{5,9},{9,13},{2,6},{6,10},{10,14},{3,7},{... | collective-permute-start | bytes 98312 | tf_op jit(solution)/shard_map/ppermute | solution.py:18
  191.8 6.0 %collective-permute-start.2 = (f32[1,16,512]{2,1,0:T(8,128)S(1)}, f32[1,16,512]{2,1,0:T(8,128)S(1)}, u32[]{:S(2)}, u32[]{:S(2)}) collective-permute-start(f32[1,16,512]{2,1,0:T(8,128)S(1)} %get-tuple-element.26), channel_id=1, source_target_pairs={{1,0},{2,1},{3,2},{5,4},{6,5},{7,6},{9,8},{10,9},{11,10},{13,12},{... | collective-permute-start | bytes 98312 | tf_op jit(solution)/shard_map/ppermute | solution.py:20
  193.1 6.1 %collective-permute-start.3 = (f32[1,16,512]{2,1,0:T(8,128)S(1)}, f32[1,16,512]{2,1,0:T(8,128)S(1)}, u32[]{:S(2)}, u32[]{:S(2)}) collective-permute-start(f32[1,16,512]{2,1,0:T(8,128)S(1)} %get-tuple-element.25), channel_id=1, source_target_pairs={{0,1},{1,2},{2,3},{4,5},{5,6},{6,7},{8,9},{9,10},{10,11},{12,13},{... | collective-permute-start | bytes 98312 | tf_op jit(solution)/shard_map/ppermute | solution.py:18
  200.4 235.0 %copy-start.3 = (f32[256,512]{1,0:T(8,128)}, f32[256,512]{1,0:T(8,128)S(1)}, u32[]{:S(2)}) copy-start(f32[256,512]{1,0:T(8,128)S(1)} %scatter_fusion) | copy-start | bytes 1572868
Sparse Core Ops, SparseCore 0:
  10.2 40.7 all-gather.6
  53.2 36.9 all-gather.4
  92.4 40.3 all-gather.8
  135.0 44.1 all-gather.10
  183.2 56.1 reduce-scatter.10
  244.0 60.6 reduce-scatter.8
  308.9 56.3 reduce-scatter.6
  370.2 65.1 reduce-scatter.4
where the time goes:
time: 443 us; the launch traced here: 442 us
  waiting for transfers between devices  296 us (67%)
  blocking collectives  63.6 us (14%)
  matrix products  29 us (7%)
  starting transfers between devices  17.8 us (4%)
  between operations  16.6 us (4%)
  local copies, waits for them, and re-layouts  10.4 us (2%)
  other arithmetic  8.89 us (2%)
    reduce_scatter x1, waiting for transfers between devices, shards(): lax.psum_scatter(inner(features, edge_grad_pre) * edge_scale, ('dom', 'su...  70.1 us
    reduce_scatter x1, waiting for transfers between devices, shards(): lax.psum_scatter(inner(node_input, node_grad_pre) * node_scale, ('dom', '...  65.3 us
    unnamed x1, blocking collectives  63.6 us
    reduce_scatter x1, waiting for transfers between devices, shards(): lax.psum_scatter(inner(edge_act, edge_grad_z) * edge_scale, ('dom', 'sub'...  60.6 us
    reduce_scatter x1, waiting for transfers between devices, shards(): lax.psum_scatter(inner(node_act, node_grad_z) * node_scale, ('dom', 'sub'...  38.9 us
    all_gather x1, waiting for transfers between devices, shards(): lax.all_gather(node_first, ('dom', 'sub'), axis=0, tiled=True)  31.2 us
    all_gather x1, waiting for transfers between devices, shards(): lax.all_gather(edge_first, ('dom', 'sub'), axis=0, tiled=True)  17.1 us
    dot_general x4, matrix products, outer_back(): lax.dot_general(left, right, (((1,), (1,)), ((), ())), precision=lax.Prec...  12.4 us
  transfers between devices with their start and end apart: 16, of which 10 were waited for; matrix products, arithmetic and copies ran while one was open for 11% of the time, Pallas kernels for 0%

commit v1 on v0

--- a/solution.py
+++ b/solution.py
@@ -1,10 +1,29 @@
+import functools
 import math
 import jax
 import jax.numpy as jnp
 from jax import lax
 from jax.sharding import PartitionSpec as P
+from jax.lax import axis_index, axis_size, ppermute
 
 EPSILON = 1e-05
+
+
+def perform_record(local_x, axis_tag):
+    carry_in, part_next, o_now = (axis_size(axis_tag), axis_index(axis_tag), local_x.shape[0])
+    a_now = range(carry_in)
+    kept_rows = list(map(lambda d: (d, (d + 1) % carry_in), a_now))
+    placed = jnp.zeros((*local_x.shape[:0], carry_in * o_now, *local_x.shape[1:]), local_x.dtype)
+    a_next = local_x
+    for src_i in [*range(carry_in)]:
+        high = (part_next - src_i) % carry_in
+        placed = lax.dynamic_update_slice_in_dim(placed, a_next, high * o_now, axis=0)
+        if src_i < carry_in - 1:
+            a_next = ppermute(a_next, axis_tag, kept_rows)
+    return placed
+
+
+trace_leaves = functools.partial(perform_record, axis_tag=("dom", "sub"))
 
 
 def padded(cells, sides, width):
@@ -94,7 +113,7 @@
     ghosts = jnp.stack([dom_side[0], dom_side[3], sub_side[0], sub_side[3]])
     ghosts = ghosts.reshape(4 * ghost, width)
     full_node_first, full_node_second, full_node_bias, full_node_gain = (
-        lax.all_gather(node_first, ("dom", "sub"), axis=0, tiled=True),
+        trace_leaves(node_first),
         lax.all_gather(node_second, ("dom", "sub"), axis=0, tiled=True),
         lax.all_gather(node_bias, ("dom", "sub"), axis=0, tiled=True),
         lax.all_gather(node_gain, ("dom", "sub"), axis=0, tiled=True),

time: 443 us -> 458 us (1.034)
  waiting for transfers between devices: 296 us -> 309 us
    ppermute x0 -> x15, waiting for transfers between devices: none -> 102 us  [perform_record(): a_next = ppermute(a_next, axis_tag, kept_rows)]
    reduce_scatter x1, waiting for transfers between devices: 60.6 us -> 3.72 us  [shards(): lax.psum_scatter(inner(edge_act, edge_grad_z) * edge_scale, ('dom', 'sub'...]
    all_gather x1 -> x0, waiting for transfers between devices: 31.2 us -> none  [shards(): lax.all_gather(node_first, ('dom', 'sub'), axis=0, tiled=True)]
    reduce_scatter x1, waiting for transfers between devices: 38.9 us -> 61 us  [shards(): lax.psum_scatter(inner(node_act, node_grad_z) * node_scale, ('dom', 'sub'...]
    all_gather x1, waiting for transfers between devices: 17.1 us -> 0.01 us  [shards(): lax.all_gather(edge_first, ('dom', 'sub'), axis=0, tiled=True)]
  transfers between devices with their start and end apart: 16 -> 30, of which waited for: 10 -> 21; matrix products, arithmetic and copies ran while one was open for 11% -> 10% of each run, Pallas kernels for 0% -> 0%
where the time goes in v1:
time: 458 us; the launch traced here: 457 us
  waiting for transfers between devices  309 us (67%)
  blocking collectives  63.1 us (14%)
  matrix products  28 us (6%)
  starting transfers between devices  19 us (4%)
  between operations  16.9 us (4%)
  local copies, waits for them, and re-layouts  11.5 us (3%)
  other arithmetic  9.88 us (2%)
    ppermute x15, waiting for transfers between devices, perform_record(): a_next = ppermute(a_next, axis_tag, kept_rows)  102 us
    reduce_scatter x1, waiting for transfers between devices, shards(): lax.psum_scatter(inner(features, edge_grad_pre) * edge_scale, ('dom', 'su...  70.1 us
    reduce_scatter x1, waiting for transfers between devices, shards(): lax.psum_scatter(inner(node_input, node_grad_pre) * node_scale, ('dom', '...  64.8 us
    unnamed x1, blocking collectives  63.1 us
    reduce_scatter x1, waiting for transfers between devices, shards(): lax.psum_scatter(inner(node_act, node_grad_z) * node_scale, ('dom', 'sub'...  61 us
    dot_general x4, matrix products, inner(): lax.dot_general(left, right, (((0,), (0,)), ((), ())), precision=lax.Prec...  12.1 us
    dot_general x4, matrix products, outer_back(): lax.dot_general(left, right, (((1,), (1,)), ((), ())), precision=lax.Prec...  11.3 us
    ppermute x4, starting transfers between devices, padded(): lax.ppermute(tail, axis, [(i, (i + 1) % count) for i in range(ends)])  10.2 us
  transfers between devices with their start and end apart: 30, of which 21 were waited for; matrix products, arithmetic and copies ran while one was open for 10% of the time, Pallas kernels for 0%

profile of v1, /device:TPU:0, one launch (start us, length us, event | category | flops | bytes accessed | tf_op | source)
XLA Modules:
  0.0 457.3 jit_solution(10529985435853808612)
XLA Ops:
  8.7 3.1 collective-permute-start
  11.8 5.8 %collective-permute-done = f32[64,512]{1,0:T(8,128)S(1)} collective-permute-done((f32[64,512]{1,0:T(8,128)}, f32[64,512]{1,0:T(8,128)S(1)}, u32[]{:S(2)}, u32[]{:S(2)}) %collective-permute-start) | collective-permute-done | bytes 131104 | tf_op jit(solution)/shard_map/ppermute | solution.py:22
  17.6 8.4 %collective-permute-done.1 = f32[64,512]{1,0:T(8,128)S(1)} collective-permute-done((f32[64,512]{1,0:T(8,128)S(1)}, f32[64,512]{1,0:T(8,128)S(1)}, u32[]{:S(2)}, u32[]{:S(2)}) %collective-permute-start.1) | collective-permute-done | bytes 131104 | tf_op jit(solution)/shard_map/ppermute | solution.py:22
  26.0 8.6 %collective-permute-done.2 = f32[64,512]{1,0:T(8,128)S(1)} collective-permute-done((f32[64,512]{1,0:T(8,128)S(1)}, f32[64,512]{1,0:T(8,128)S(1)}, u32[]{:S(2)}, u32[]{:S(2)}) %collective-permute-start.2) | collective-permute-done | bytes 131104 | tf_op jit(solution)/shard_map/ppermute | solution.py:22
  34.7 7.4 %collective-permute-done.3 = f32[64,512]{1,0:T(8,128)S(1)} collective-permute-done((f32[64,512]{1,0:T(8,128)S(1)}, f32[64,512]{1,0:T(8,128)S(1)}, u32[]{:S(2)}, u32[]{:S(2)}) %collective-permute-start.3) | collective-permute-done | bytes 131104 | tf_op jit(solution)/shard_map/ppermute | solution.py:22
  42.2 1.3 compare_and_fusion.1
  43.5 7.4 %collective-permute-done.4 = f32[64,512]{1,0:T(8,128)S(1)} collective-permute-done((f32[64,512]{1,0:T(8,128)S(1)}, f32[64,512]{1,0:T(8,128)S(1)}, u32[]{:S(2)}, u32[]{:S(2)}) %collective-permute-start.4) | collective-permute-done | bytes 131104 | tf_op jit(solution)/shard_map/ppermute | solution.py:22
  52.9 5.1 %collective-permute-done.5 = f32[64,512]{1,0:T(8,128)S(1)} collective-permute-done((f32[64,512]{1,0:T(8,128)S(1)}, f32[64,512]{1,0:T(8,128)S(1)}, u32[]{:S(2)}, u32[]{:S(2)}) %collective-permute-start.5) | collective-permute-done | bytes 131104 | tf_op jit(solution)/shard_map/ppermute | solution.py:22
  58.0 7.1 %collective-permute-done.6 = f32[64,512]{1,0:T(8,128)S(1)} collective-permute-done((f32[64,512]{1,0:T(8,128)S(1)}, f32[64,512]{1,0:T(8,128)S(1)}, u32[]{:S(2)}, u32[]{:S(2)}) %collective-permute-start.6) | collective-permute-done | bytes 131104 | tf_op jit(solution)/shard_map/ppermute | solution.py:22
  65.2 1.2 dynamic-slice
  67.1 0.9 dynamic-update-slice
  69.6 0.8 dynamic-update-slice.3
  71.3 63.1 %all-reduce.5 = (f32[512]{0:T(512)S(1)}, f32[512]{0:T(512)S(1)}, f32[512]{0:T(512)S(1)}, f32[512]{0:T(512)S(1)}, f32[512]{0:T(512)S(1)}) all-reduce(f32[512]{0:T(512)S(1)} %dynamic-update-slice.1, f32[512]{0:T(512)S(1)} %dynamic-update-slice.2, f32[512]{0:T(512)S(1)} %dynamic-update-slice.3, ...), channel_id=1, replica_groups=mesh['groups'=2,'dom'=4,'sub'=4] {'dom','sub'}, use_global_device_ids=true, to_apply=%add.1 | all-reduce | flops 2560 | bytes 20480
  134.8 7.0 %collective-permute-done.8 = f32[64,512]{1,0:T(8,128)S(1)} collective-permute-done((f32[64,512]{1,0:T(8,128)S(1)}, f32[64,512]{1,0:T(8,128)S(1)}, u32[]{:S(2)}, u32[]{:S(2)}) %collective-permute-start.8) | collective-permute-done | bytes 131104 | tf_op jit(solution)/shard_map/ppermute | solution.py:22
  141.9 7.0 %collective-permute-done.9 = f32[64,512]{1,0:T(8,128)S(1)} collective-permute-done((f32[64,512]{1,0:T(8,128)S(1)}, f32[64,512]{1,0:T(8,128)S(1)}, u32[]{:S(2)}, u32[]{:S(2)}) %collective-permute-start.9) | collective-permute-done | bytes 131104 | tf_op jit(solution)/shard_map/ppermute | solution.py:22
  149.0 7.0 %collective-permute-done.10 = f32[64,512]{1,0:T(8,128)S(1)} collective-permute-done((f32[64,512]{1,0:T(8,128)S(1)}, f32[64,512]{1,0:T(8,128)S(1)}, u32[]{:S(2)}, u32[]{:S(2)}) %collective-permute-start.10) | collective-permute-done | bytes 131104 | tf_op jit(solution)/shard_map/ppermute | solution.py:22
  156.1 7.7 %collective-permute-done.11 = f32[64,512]{1,0:T(8,128)S(1)} collective-permute-done((f32[64,512]{1,0:T(8,128)S(1)}, f32[64,512]{1,0:T(8,128)S(1)}, u32[]{:S(2)}, u32[]{:S(2)}) %collective-permute-start.11) | collective-permute-done | bytes 131104 | tf_op jit(solution)/shard_map/ppermute | solution.py:22
  163.9 8.3 %collective-permute-done.12 = f32[64,512]{1,0:T(8,128)S(1)} collective-permute-done((f32[64,512]{1,0:T(8,128)S(1)}, f32[64,512]{1,0:T(8,128)S(1)}, u32[]{:S(2)}, u32[]{:S(2)}) %collective-permute-start.12) | collective-permute-done | bytes 131104 | tf_op jit(solution)/shard_map/ppermute | solution.py:22
  172.2 7.4 %collective-permute-done.13 = f32[64,512]{1,0:T(8,128)S(1)} collective-permute-done((f32[64,512]{1,0:T(8,128)S(1)}, f32[64,512]{1,0:T(8,128)S(1)}, u32[]{:S(2)}, u32[]{:S(2)}) %collective-permute-start.13) | collective-permute-done | bytes 131104 | tf_op jit(solution)/shard_map/ppermute | solution.py:22
  179.6 7.0 %collective-permute-done.14 = f32[64,512]{1,0:T(8,128)S(1)} collective-permute-done((f32[64,512]{1,0:T(8,128)S(1)}, f32[64,512]{1,0:T(8,128)S(1)}, u32[]{:S(2)}, u32[]{:S(2)}) %collective-permute-start.14) | collective-permute-done | bytes 131104 | tf_op jit(solution)/shard_map/ppermute | solution.py:22
  186.7 2.6 fusion.44
  189.9 2.3 convolution_select_fusion
  192.1 1.9 fusion.45
  194.1 1.0 copy-done.7
  196.1 2.0 fusion.43
  198.6 2.1 convolution_multiply_fusion.3
  201.0 2.3 convolution_multiply_fusion.2
  204.0 1.6 scatter_custom_fusion.2
  205.6 3.2 convolution_multiply_fusion.1
  209.9 1.3 collective-permute-start.19
  211.2 1.3 collective-permute-start.20
  212.5 1.3 collective-permute-start.21
  213.8 1.3 collective-permute-start.22
  215.3 4.4 collective-permute-done.22
  222.2 1.9 convolution_select_fusion.1
  224.1 4.4 convolution_multiply_fusion
  229.2 5.3 %fusion.46 = f32[128,1536]{1,0:T(8,128)S(1)} fusion(f32[128,512]{1,0:T(8,128)S(1)} %convolution_select_fusion.1, f32[1536,512]{1,0:T(8,128)} %all-gather.8.cloned.1.call-done), kind=kOutput, calls=%fused_computation.131 | convolution fusion | flops 1207959552 | bytes 4194304 | tf_op jit(solution)/shard_map/dot_general | solution.py:61
  235.3 2.3 scatter_custom_fusion
  237.6 1.3 collective-permute-start.15
  238.9 3.0 collective-permute-start.16
  241.9 1.3 collective-permute-start.17
  243.2 4.5 collective-permute-start.18
  247.9 1.7 collective-permute-done.18
  249.6 1.2 scatter_fusion
  250.8 3.7 reduce-scatter.7.cloned.1.call-done
  254.6 61.0 %reduce-scatter.11.cloned.1.call-done = f32[32,512]{1,0:T(8,128)} async-done(((f32[512,512]{1,0:T(8,128)}), f32[32,512]{1,0:T(8,128)}) %reduce-scatter.11.cloned.1.call-update) | async-done | bytes 65552 | tf_op jit(solution)/shard_map/reduce_scatter | solution.py:151
  315.5 64.8 %reduce-scatter.9.cloned.1.call-done = f32[64,512]{1,0:T(8,128)} async-done(((f32[1024,512]{1,0:T(8,128)}), f32[64,512]{1,0:T(8,128)}) %reduce-scatter.9.cloned.1.call-update) | async-done | bytes 131088 | tf_op jit(solution)/shard_map/reduce_scatter | solution.py:145
  380.4 70.1 %reduce-scatter.5.cloned.1.call-done = f32[96,512]{1,0:T(8,128)} async-done(((f32[1536,512]{1,0:T(8,128)}), f32[96,512]{1,0:T(8,128)}) %reduce-scatter.5.cloned.1.call-update) | async-done | bytes 196624 | tf_op jit(solution)/shard_map/reduce_scatter | solution.py:173
  (152 shorter events, 13.4 us)
Async XLA Ops:
  7.2 127.5 %copy-start.15 = (f32[64,512]{1,0:T(8,128)S(1)}, f32[64,512]{1,0:T(8,128)}, u32[]{:S(2)}) copy-start(f32[64,512]{1,0:T(8,128)} %param.36) | copy-start | bytes 393220
  7.2 179.5 %all-gather.6.cloned.1.call-start = ((), (), s32[]{:S(2)}) async-start(), calls=%async_computation.5 | async-start | bytes 1114112 | tf_op jit(solution)/shard_map/all_gather | solution.py:117
  7.9 188.0 %all-gather.4.cloned.1.call-start = ((), (), s32[]{:S(2)}) async-start(), calls=%async_computation.4 | async-start | bytes 1114112 | tf_op jit(solution)/shard_map/all_gather | solution.py:123
  8.7 220.5 %all-gather.8.cloned.1.call-start = ((), (), s32[]{:S(2)}) async-start(), calls=%async_computation.6 | async-start | bytes 3342336 | tf_op jit(solution)/shard_map/all_gather | solution.py:122
  8.7 8.9 %collective-permute-start = (f32[64,512]{1,0:T(8,128)}, f32[64,512]{1,0:T(8,128)S(1)}, u32[]{:S(2)}, u32[]{:S(2)}) collective-permute-start(f32[64,512]{1,0:T(8,128)} %param.36), channel_id=1, source_target_pairs={{0,1},{1,2},{2,3},{3,4},{4,5},{5,6},{6,7},{7,8},{8,9},{9,10},{10,1... | collective-permute-start | bytes 393224 | tf_op jit(solution)/shard_map/ppermute | solution.py:22
  17.6 8.4 %collective-permute-start.1 = (f32[64,512]{1,0:T(8,128)S(1)}, f32[64,512]{1,0:T(8,128)S(1)}, u32[]{:S(2)}, u32[]{:S(2)}) collective-permute-start(f32[64,512]{1,0:T(8,128)S(1)} %collective-permute-done), channel_id=1, source_target_pairs={{0,1},{1,2},{2,3},{3,4},{4,5},{5,6},{6,7},{7,8},{8,9},{9,10},{10,1... | collective-permute-start | bytes 393224 | tf_op jit(solution)/shard_map/ppermute | solution.py:22
  26.0 8.6 %collective-permute-start.2 = (f32[64,512]{1,0:T(8,128)S(1)}, f32[64,512]{1,0:T(8,128)S(1)}, u32[]{:S(2)}, u32[]{:S(2)}) collective-permute-start(f32[64,512]{1,0:T(8,128)S(1)} %collective-permute-done.1), channel_id=1, source_target_pairs={{0,1},{1,2},{2,3},{3,4},{4,5},{5,6},{6,7},{7,8},{8,9},{9,10},{10,1... | collective-permute-start | bytes 393224 | tf_op jit(solution)/shard_map/ppermute | solution.py:22
  34.7 7.5 %collective-permute-start.3 = (f32[64,512]{1,0:T(8,128)S(1)}, f32[64,512]{1,0:T(8,128)S(1)}, u32[]{:S(2)}, u32[]{:S(2)}) collective-permute-start(f32[64,512]{1,0:T(8,128)S(1)} %collective-permute-done.2), channel_id=1, source_target_pairs={{0,1},{1,2},{2,3},{3,4},{4,5},{5,6},{6,7},{7,8},{8,9},{9,10},{10,1... | collective-permute-start | bytes 393224 | tf_op jit(solution)/shard_map/ppermute | solution.py:22
  34.7 219.9 %reduce-scatter.7.cloned.1.call-start = ((), (), s32[]{:S(2)}) async-start(), calls=%async_computation.8 | async-start | bytes 1114112 | tf_op jit(solution)/shard_map/reduce_scatter | solution.py:165
  42.2 8.7 %collective-permute-start.4 = (f32[64,512]{1,0:T(8,128)S(1)}, f32[64,512]{1,0:T(8,128)S(1)}, u32[]{:S(2)}, u32[]{:S(2)}) collective-permute-start(f32[64,512]{1,0:T(8,128)S(1)} %collective-permute-done.3), channel_id=1, source_target_pairs={{0,1},{1,2},{2,3},{3,4},{4,5},{5,6},{6,7},{7,8},{8,9},{9,10},{10,1... | collective-permute-start | bytes 393224 | tf_op jit(solution)/shard_map/ppermute | solution.py:22
  50.9 7.1 %collective-permute-start.5 = (f32[64,512]{1,0:T(8,128)S(1)}, f32[64,512]{1,0:T(8,128)S(1)}, u32[]{:S(2)}, u32[]{:S(2)}) collective-permute-start(f32[64,512]{1,0:T(8,128)S(1)} %collective-permute-done.4), channel_id=1, source_target_pairs={{0,1},{1,2},{2,3},{3,4},{4,5},{5,6},{6,7},{7,8},{8,9},{9,10},{10,1... | collective-permute-start | bytes 393224 | tf_op jit(solution)/shard_map/ppermute | solution.py:22
  58.0 7.2 %collective-permute-start.6 = (f32[64,512]{1,0:T(8,128)S(1)}, f32[64,512]{1,0:T(8,128)S(1)}, u32[]{:S(2)}, u32[]{:S(2)}) collective-permute-start(f32[64,512]{1,0:T(8,128)S(1)} %collective-permute-done.5), channel_id=1, source_target_pairs={{0,1},{1,2},{2,3},{3,4},{4,5},{5,6},{6,7},{7,8},{8,9},{9,10},{10,1... | collective-permute-start | bytes 393224 | tf_op jit(solution)/shard_map/ppermute | solution.py:22
  58.0 146.0 %copy-start.17 = (f32[128]{0:T(128)}, f32[128]{0:T(128)S(1)}, u32[]{:S(2)}) copy-start(f32[128]{0:T(128)S(1)} %compare_convert_fusion) | copy-start | bytes 1540
  65.2 69.5 %collective-permute-start.7 = (f32[64,512]{1,0:T(8,128)S(1)}, f32[64,512]{1,0:T(8,128)S(1)}, u32[]{:S(2)}, u32[]{:S(2)}) collective-permute-start(f32[64,512]{1,0:T(8,128)S(1)} %collective-permute-done.6), channel_id=1, source_target_pairs={{0,1},{1,2},{2,3},{3,4},{4,5},{5,6},{6,7},{7,8},{8,9},{9,10},{10,1... | collective-permute-start | bytes 393224 | tf_op jit(solution)/shard_map/ppermute | solution.py:22
  134.7 7.1 %collective-permute-start.8 = (f32[64,512]{1,0:T(8,128)S(1)}, f32[64,512]{1,0:T(8,128)S(1)}, u32[]{:S(2)}, u32[]{:S(2)}) collective-permute-start(f32[64,512]{1,0:T(8,128)S(1)} %collective-permute-done.7), channel_id=1, source_target_pairs={{0,1},{1,2},{2,3},{3,4},{4,5},{5,6},{6,7},{7,8},{8,9},{9,10},{10,1... | collective-permute-start | bytes 393224 | tf_op jit(solution)/shard_map/ppermute | solution.py:22
  141.9 7.1 %collective-permute-start.9 = (f32[64,512]{1,0:T(8,128)S(1)}, f32[64,512]{1,0:T(8,128)S(1)}, u32[]{:S(2)}, u32[]{:S(2)}) collective-permute-start(f32[64,512]{1,0:T(8,128)S(1)} %collective-permute-done.8), channel_id=1, source_target_pairs={{0,1},{1,2},{2,3},{3,4},{4,5},{5,6},{6,7},{7,8},{8,9},{9,10},{10,1... | collective-permute-start | bytes 393224 | tf_op jit(solution)/shard_map/ppermute | solution.py:22
  149.0 7.1 %collective-permute-start.10 = (f32[64,512]{1,0:T(8,128)S(1)}, f32[64,512]{1,0:T(8,128)S(1)}, u32[]{:S(2)}, u32[]{:S(2)}) collective-permute-start(f32[64,512]{1,0:T(8,128)S(1)} %collective-permute-done.9), channel_id=1, source_target_pairs={{0,1},{1,2},{2,3},{3,4},{4,5},{5,6},{6,7},{7,8},{8,9},{9,10},{10,1... | collective-permute-start | bytes 393224 | tf_op jit(solution)/shard_map/ppermute | solution.py:22
  156.0 7.8 %collective-permute-start.11 = (f32[64,512]{1,0:T(8,128)S(1)}, f32[64,512]{1,0:T(8,128)S(1)}, u32[]{:S(2)}, u32[]{:S(2)}) collective-permute-start(f32[64,512]{1,0:T(8,128)S(1)} %collective-permute-done.10), channel_id=1, source_target_pairs={{0,1},{1,2},{2,3},{3,4},{4,5},{5,6},{6,7},{7,8},{8,9},{9,10},{10,1... | collective-permute-start | bytes 393224 | tf_op jit(solution)/shard_map/ppermute | solution.py:22
  163.8 8.3 %collective-permute-start.12 = (f32[64,512]{1,0:T(8,128)S(1)}, f32[64,512]{1,0:T(8,128)S(1)}, u32[]{:S(2)}, u32[]{:S(2)}) collective-permute-start(f32[64,512]{1,0:T(8,128)S(1)} %collective-permute-done.11), channel_id=1, source_target_pairs={{0,1},{1,2},{2,3},{3,4},{4,5},{5,6},{6,7},{7,8},{8,9},{9,10},{10,1... | collective-permute-start | bytes 393224 | tf_op jit(solution)/shard_map/ppermute | solution.py:22
  163.8 25.7 %copy-start.1 = (f32[256,512]{1,0:T(8,128)S(1)}, f32[256,512]{1,0:T(8,128)}, u32[]{:S(2)}) copy-start(f32[256,512]{1,0:T(8,128)} %param.25) | copy-start | bytes 1572868
  172.1 7.4 %collective-permute-start.13 = (f32[64,512]{1,0:T(8,128)S(1)}, f32[64,512]{1,0:T(8,128)S(1)}, u32[]{:S(2)}, u32[]{:S(2)}) collective-permute-start(f32[64,512]{1,0:T(8,128)S(1)} %collective-permute-done.12), channel_id=1, source_target_pairs={{0,1},{1,2},{2,3},{3,4},{4,5},{5,6},{6,7},{7,8},{8,9},{9,10},{10,1... | collective-permute-start | bytes 393224 | tf_op jit(solution)/shard_map/ppermute | solution.py:22
  179.6 7.1 %collective-permute-start.14 = (f32[64,512]{1,0:T(8,128)S(1)}, f32[64,512]{1,0:T(8,128)S(1)}, u32[]{:S(2)}, u32[]{:S(2)}) collective-permute-start(f32[64,512]{1,0:T(8,128)S(1)} %collective-permute-done.13), channel_id=1, source_target_pairs={{0,1},{1,2},{2,3},{3,4},{4,5},{5,6},{6,7},{7,8},{8,9},{9,10},{10,1... | collective-permute-start | bytes 393224 | tf_op jit(solution)/shard_map/ppermute | solution.py:22
  186.7 3.2 copy-start.9
  195.2 3.2 copy-start.12
  198.1 2.9 copy-start.4
  198.6 4.8 %copy-start.20 = (f32[128]{0:T(128)}, f32[128]{0:T(128)S(1)}, u32[]{:S(2)}) copy-start(f32[128]{0:T(128)S(1)} %broadcast_multiply_fusion.3) | copy-start | bytes 1540
  200.8 2.6 copy-start.19
  200.8 4.8 %copy-start = (f32[256,512]{1,0:T(8,128)S(1)}, f32[256,512]{1,0:T(8,128)}, u32[]{:S(2)}) copy-start(f32[256,512]{1,0:T(8,128)} %param.21) | copy-start | bytes 1572868
  200.8 4.8 %copy-start.3 = (f32[256,512]{1,0:T(8,128)S(1)}, f32[256,512]{1,0:T(8,128)}, u32[]{:S(2)}) copy-start(f32[256,512]{1,0:T(8,128)} %copy-done.2) | copy-start | bytes 1572868
  200.8 114.7 %reduce-scatter.11.cloned.1.call-start = ((), (), s32[]{:S(2)}) async-start(), calls=%async_computation.10 | async-start | bytes 1114112 | tf_op jit(solution)/shard_map/reduce_scatter | solution.py:151
  203.4 177.0 %reduce-scatter.9.cloned.1.call-start = ((), (), s32[]{:S(2)}) async-start(), calls=%async_computation.9 | async-start | bytes 2228224 | tf_op jit(solution)/shard_map/reduce_scatter | solution.py:145
  205.6 3.3 copy-start.16
  208.8 241.6 %reduce-scatter.5.cloned.1.call-start = ((), (), s32[]{:S(2)}) async-start(), calls=%async_computation.7 | async-start | bytes 3342336 | tf_op jit(solution)/shard_map/reduce_scatter | solution.py:173
  209.0 10.8 %copy-start.22 = (s32[64]{0:T(128)}, s32[64]{0:T(128)S(1)}, u32[]{:S(2)}) copy-start(s32[64]{0:T(128)S(1)} %reshape.204) | copy-start | bytes 772
  209.9 5.2 %collective-permute-start.19 = (f32[1,16,512]{2,1,0:T(8,128)S(1)}, f32[1,16,512]{2,1,0:T(8,128)S(1)}, u32[]{:S(2)}, u32[]{:S(2)}) collective-permute-start(f32[1,16,512]{2,1,0:T(8,128)S(1)} %get-tuple-element.28), channel_id=1, source_target_pairs={{0,4},{4,8},{8,12},{1,5},{5,9},{9,13},{2,6},{6,10},{10,14},{3,7},{... | collective-permute-start | bytes 98312 | tf_op jit(solution)/shard_map/ppermute | solution.py:37
  211.2 3.9 collective-permute-start.20
  212.5 2.9 collective-permute-start.21
  213.8 6.0 %collective-permute-start.22 = (f32[1,16,512]{2,1,0:T(8,128)S(1)}, f32[1,16,512]{2,1,0:T(8,128)S(1)}, u32[]{:S(2)}, u32[]{:S(2)}) collective-permute-start(f32[1,16,512]{2,1,0:T(8,128)S(1)} %get-tuple-element.29), channel_id=1, source_target_pairs={{1,0},{2,1},{3,2},{5,4},{6,5},{7,6},{9,8},{10,9},{11,10},{13,12},{... | collective-permute-start | bytes 98312 | tf_op jit(solution)/shard_map/ppermute | solution.py:39
  221.4 2.7 copy-start.14
  229.1 5.3 %copy-start.13 = (f32[128,512]{1,0:T(8,128)S(1)}, f32[128,512]{1,0:T(8,128)}, u32[]{:S(2)}) copy-start(f32[128,512]{1,0:T(8,128)} %param.26) | copy-start | bytes 786436
  229.2 5.3 %copy-start.18 = (f32[128]{0:T(128)S(1)}, f32[128]{0:T(128)}, u32[]{:S(2)}) copy-start(f32[128]{0:T(128)} %copy-done.17) | copy-start | bytes 1540
  234.5 13.3 %copy-start.8 = (f32[256,1024]{1,0:T(8,128)S(1)}, f32[256,1024]{1,0:T(8,128)}, u32[]{:S(2)}) copy-start(f32[256,1024]{1,0:T(8,128)} %copy-done.7) | copy-start | bytes 3145732
  235.3 14.4 %copy-start.23 = (s32[64]{0:T(128)S(1)}, s32[64]{0:T(128)}, u32[]{:S(2)}) copy-start(s32[64]{0:T(128)} %copy-done.22) | copy-start | bytes 772
  237.6 10.3 %collective-permute-start.15 = (f32[1,16,512]{2,1,0:T(8,128)S(1)}, f32[1,16,512]{2,1,0:T(8,128)S(1)}, u32[]{:S(2)}, u32[]{:S(2)}) collective-permute-start(f32[1,16,512]{2,1,0:T(8,128)S(1)} %get-tuple-element.24), channel_id=1, source_target_pairs={{4,0},{8,4},{12,8},{5,1},{9,5},{13,9},{6,2},{10,6},{14,10},{7,3},{... | collective-permute-start | bytes 98312 | tf_op jit(solution)/shard_map/ppermute | solution.py:39
  238.9 9.1 %collective-permute-start.16 = (f32[1,16,512]{2,1,0:T(8,128)S(1)}, f32[1,16,512]{2,1,0:T(8,128)S(1)}, u32[]{:S(2)}, u32[]{:S(2)}) collective-permute-start(f32[1,16,512]{2,1,0:T(8,128)S(1)} %get-tuple-element.27), channel_id=1, source_target_pairs={{0,4},{4,8},{8,12},{1,5},{5,9},{9,13},{2,6},{6,10},{10,14},{3,7},{... | collective-permute-start | bytes 98312 | tf_op jit(solution)/shard_map/ppermute | solution.py:37
  241.9 6.0 %collective-permute-start.17 = (f32[1,16,512]{2,1,0:T(8,128)S(1)}, f32[1,16,512]{2,1,0:T(8,128)S(1)}, u32[]{:S(2)}, u32[]{:S(2)}) collective-permute-start(f32[1,16,512]{2,1,0:T(8,128)S(1)} %get-tuple-element.26), channel_id=1, source_target_pairs={{1,0},{2,1},{3,2},{5,4},{6,5},{7,6},{9,8},{10,9},{11,10},{13,12},{... | collective-permute-start | bytes 98312 | tf_op jit(solution)/shard_map/ppermute | solution.py:39
  243.2 6.4 %collective-permute-start.18 = (f32[1,16,512]{2,1,0:T(8,128)S(1)}, f32[1,16,512]{2,1,0:T(8,128)S(1)}, u32[]{:S(2)}, u32[]{:S(2)}) collective-permute-start(f32[1,16,512]{2,1,0:T(8,128)S(1)} %get-tuple-element.25), channel_id=1, source_target_pairs={{0,1},{1,2},{2,3},{4,5},{5,6},{6,7},{8,9},{9,10},{10,11},{12,13},{... | collective-permute-start | bytes 98312 | tf_op jit(solution)/shard_map/ppermute | solution.py:37
  250.8 199.6 %copy-start.5 = (f32[256,512]{1,0:T(8,128)}, f32[256,512]{1,0:T(8,128)S(1)}, u32[]{:S(2)}) copy-start(f32[256,512]{1,0:T(8,128)S(1)} %scatter_fusion) | copy-start | bytes 1572868
  (8 other events, 10.5 us)
Sparse Core Ops, SparseCore 0:
  10.2 42.8 all-gather.5
  55.3 36.5 all-gather.3
  94.2 44.7 all-gather.7
  200.9 53.6 reduce-scatter.6
  259.0 56.4 reduce-scatter.10
  319.7 60.6 reduce-scatter.8
  385.2 65.1 reduce-scatter.4
